TPU v7x, 32 devices: a whole 2x2x4 slice. The times are simulated.
32 devices in a mesh: row: 2 (over x), col: 4 (over z), tok: 4 (over y, core).
Axes of the slice: x: 2, y: 2, z: 4, core: 2. Of those that a mesh axis runs over, the one named last changes fastest.
Arguments:
- activations: bfloat16 [4096, 2048], P(('row', 'col', 'tok')), may hold values from -6 to 6
- norm_gain: float32 [2048], replicated, may hold values from 0.1 to 1.9
- routes: int32 [4096, 8], P(('row', 'col', 'tok')), may hold values from 0 to 127, all different within a row; in each aligned block of 128 rows (0 to 127, 128 to 255, ...) at most 10 rows name the same one
- route_weights: float32 [4096, 8], P(('row', 'col', 'tok')), may hold values from 0.05 to 1
- gate_up_weight: bfloat16 [128, 2, 768, 2048], P(('row', 'col'), None, 'tok'), may hold values from -0.125 to 0.125
- down_weight: bfloat16 [128, 768, 2048], P(('row', 'col'), 'tok'), may hold values from -0.21875 to 0.21875
Outputs:
- expert_mix: bfloat16 [4096, 2048], P(('row', 'col', 'tok'))
Inputs may be any that keep to these rules, and one draw needn't show every extreme that they name: `routes`: within the rows of one device no expert is named by more than 10 rows, a bound that some block reaches.
All inputs are finite; a program needn't handle non-finite values.
Results may differ from a plain program's by a relative error of at most 0.0085.
Values may be sent and summed in bfloat16 or wider, within the bound.
No kernel may reach another device: no remote copies, remote signals or barrier semaphores. Data moves between devices by JAX's collectives and lax.ppermute only.
A program may use at most 384 MiB of HBM per device.

v0:
```python
import math
import jax
import jax.numpy as jnp
from jax import lax
from jax.sharding import PartitionSpec as P

CAP = 10
PIECES = 4
EPSILON = 1e-06
ALL = ("row", "col", "tok")


def rank_in_block(block_routes, experts):
    onehot = (block_routes[:, None] == jnp.arange(experts, dtype=jnp.int32)[None, :]).astype(
        jnp.int32
    )
    before = jnp.cumsum(onehot, axis=0) - onehot
    return jnp.sum(before * onehot, axis=1)


def rms_normed(activations, norm_gain):
    values = activations.astype(jnp.float32)
    scale = lax.rsqrt(jnp.mean(values * values, axis=-1, keepdims=True) + EPSILON)
    return (values * scale * norm_gain).astype(jnp.bfloat16)


def local(activations, norm_gain, routes, route_weights, gate_up_weight, down_weight):
    count, features = activations.shape
    chosen = routes.shape[1]
    holding = gate_up_weight.shape[0]
    row_count = lax.axis_size("row")
    col_count = lax.axis_size("col")
    tok_count = lax.axis_size("tok")
    owners = row_count * col_count
    experts = holding * owners
    devices = owners * tok_count
    owner = lax.axis_index("row") * col_count + lax.axis_index("col")
    assert count < 256
    normed = rms_normed(activations, norm_gain)
    gates = route_weights / jnp.sum(route_weights, axis=1, keepdims=True)
    flat_routes = routes.reshape(-1)
    target = flat_routes * CAP + rank_in_block(flat_routes, experts)
    token_ids = jnp.arange(count * chosen, dtype=jnp.int32) // chosen
    source = jnp.full((experts * CAP,), count, jnp.int32).at[target].set(token_ids)
    extra = -(-(experts * CAP) // features)
    extra = -(-extra // 8) * 8
    stride = count + extra
    table_rows = jnp.zeros((extra * features,), jnp.bfloat16)
    table_rows = table_rows.at[: experts * CAP].set(source.astype(jnp.bfloat16))
    packed = jnp.concatenate([normed, table_rows.reshape(extra, features)], axis=0)
    every = lax.all_gather(packed, ALL, axis=0, tiled=True)
    tables = every.reshape(devices, stride, features)[:, count:, :].reshape(devices, -1)
    tables = lax.dynamic_slice_in_dim(
        tables[:, : experts * CAP], owner * holding * CAP, holding * CAP, axis=1
    ).astype(jnp.int32)
    rows = tables + (jnp.arange(devices, dtype=jnp.int32) * stride)[:, None]
    rows = rows.reshape(owners, tok_count, holding, CAP).transpose(2, 1, 0, 3).reshape(-1)
    rows = rows.reshape(holding, -1)
    pieces = math.gcd(holding, PIECES)
    width = holding // pieces
    returned = []
    sums = []
    for piece in range(pieces):
        span = slice(piece * width, (piece + 1) * width)
        picked = jnp.take(every, rows[span].reshape(-1), axis=0, mode="clip")
        picked = picked.reshape(width, tok_count * owners * CAP, features)
        both = jnp.einsum(
            "jrd,jgfd->jrgf", picked, gate_up_weight[span], preferred_element_type=jnp.float32
        )
        hidden = (jax.nn.silu(both[:, :, 0, :]) * both[:, :, 1, :]).astype(jnp.bfloat16)
        partial = jnp.einsum(
            "jrf,jfd->jrd", hidden, down_weight[span], preferred_element_type=jnp.float32
        )
        partial = partial.astype(jnp.bfloat16)
        if sums:
            partial, _ = lax.optimization_barrier((partial, (sums[-1], returned[:-1])))
        sums.append(lax.psum_scatter(partial, "tok", scatter_dimension=1, tiled=True))
        summed = sums[-1].reshape(width, owners, CAP, features).transpose(1, 0, 2, 3)
        summed = summed.reshape(owners, width * CAP, features)
        returned.append(
            lax.all_to_all(summed, ("row", "col"), split_axis=0, concat_axis=0, tiled=True)
        )
    returned = jnp.concatenate(returned, axis=1)
    picked_back = jnp.take(returned.reshape(experts * CAP, features), target, axis=0)
    picked_back = picked_back.reshape(count, chosen, features)
    mixed = jnp.einsum("tk,tkd->td", gates, picked_back.astype(jnp.float32))
    return mixed.astype(jnp.bfloat16)


def solution(mesh):
    in_specs = (
        P(("row", "col", "tok"), None),
        P(),
        P(("row", "col", "tok"), None),
        P(("row", "col", "tok"), None),
        P(("row", "col"), None, "tok", None),
        P(("row", "col"), "tok", None),
    )
    out_specs = P(("row", "col", "tok"), None)
    return jax.shard_map(local, mesh=mesh, in_specs=in_specs, out_specs=out_specs, check_vma=False)
```

profile of v0, /device:TPU:0, one launch (start us, length us, event | category | flops | bytes accessed | tf_op | source)
XLA Modules:
  0.0 457.8 jit_solution(16420601011597710427)
XLA Ops:
  16.2 122.6 %all-gather.2.cloned.1.call-done = bf16[4352,2048]{1,0:T(8,128)(2,1)} async-done(((bf16[136,2048]{1,0:T(8,128)(2,1)}), bf16[4352,2048]{1,0:T(8,128)(2,1)}) %all-gather.2.cloned.1.call-update) | async-done | bytes 17825808 | tf_op jit(solution)/shard_map/all_gather | solution.py:51
  141.2 19.2 %gather_fusion = bf16[1280,2048]{1,0:T(8,128)(2,1)} fusion(bf16[4352,2048]{1,0:T(8,128)(2,1)} %all-gather.2.cloned.1.call-done, s32[2048]{0:T(1024)S(1)} %pad_clamp_fusion.3), kind=kCustom, calls=%fused_computation | custom fusion | bytes 10490880 | tf_op jit(solution)/shard_map/jit(_take)/gather | solution.py:65
  160.4 7.8 %fusion.6 = f32[4,320,2,192]{1,3,2,0:T(8,128)S(1)} fusion(bf16[4,320,2048,1]{2,1,3,0:T(8,128)(2,1)} %bitcast.124, bf16[16,2,192,2048]{3,2,1,0:T(8,128)(2,1)} %param.12), kind=kOutput, calls=%fused_computation.12 | convolution fusion | flops 2013265920 | bytes 13500416 | tf_op jit(solution)/shard_map/jrd,jgfd->jrgf/dot_general | solution.py:67
  168.2 5.8 %convolution_convert_fusion.3 = bf16[4,320,2048]{2,1,0:T(8,128)(2,1)} fusion(bf16[16,192,2048]{2,1,0:T(8,128)(2,1)} %param.13, f32[4,320,2,192]{1,3,2,0:T(8,128)S(1)} %fusion.6), kind=kOutput, calls=%fused_computation.21 | convolution fusion | flops 1010728960 | bytes 10354688 | tf_op jit(solution)/shard_map/jrf,jfd->jrd/dot_general | solution.py:71
  174.2 16.3 %fusion.49 = (bf16[4,2,192,2048]{3,2,1,0:T(8,128)(2,1)}, bf16[4,2,192,2048]{3,2,1,0:T(8,128)(2,1)}, bf16[4,2,192,2048]{3,2,1,0:T(8,128)(2,1)}) fusion(bf16[16,2,192,2048]{3,2,1,0:T(8,128)(2,1)} %param.12), kind=kLoop, calls=%fused_computation.91 | loop fusion | bytes 37748736 | tf_op jit(solution)/shard_map/slice | solution.py:68
  190.6 20.0 %gather_fusion.1 = bf16[1280,2048]{1,0:T(8,128)(2,1)} fusion(bf16[4352,2048]{1,0:T(8,128)(2,1)} %all-gather.2.cloned.1.call-done, s32[2048]{0:T(1024)S(1)} %pad_clamp_fusion.2), kind=kCustom, calls=%fused_computation.1 | custom fusion | bytes 10490880 | tf_op jit(solution)/shard_map/jit(_take)/gather | solution.py:65
  210.7 7.8 %fusion.4 = f32[4,320,2,192]{1,3,0,2:T(8,128)S(1)} fusion(bf16[4,320,2048,1]{2,1,0,3:T(8,128)(2,1)} %bitcast.122, bf16[4,2,192,2048]{3,2,1,0:T(8,128)(2,1)} %get-tuple-element.23), kind=kOutput, calls=%fused_computation.10 | convolution fusion | flops 2013265920 | bytes 13500416 | tf_op jit(solution)/shard_map/jrd,jgfd->jrgf/dot_general | solution.py:67
  218.5 5.8 %convolution_convert_fusion.2 = bf16[4,320,2048]{2,1,0:T(8,128)(2,1)} fusion(bf16[16,192,2048]{2,1,0:T(8,128)(2,1)} %param.13, f32[4,320,2,192]{1,3,0,2:T(8,128)S(1)} %fusion.4), kind=kOutput, calls=%fused_computation.20 | convolution fusion | flops 1010728960 | bytes 10354688 | tf_op jit(solution)/shard_map/jrf,jfd->jrd/dot_general | solution.py:71
  229.1 5.0 %all-to-all-start = ((bf16[8,40,2048]{2,1,0:T(8,128)(2,1)}), bf16[8,40,2048]{2,1,0:T(8,128)(2,1)S(1)}, u32[]{:S(2)}, u32[]{:S(2)}) async-start(bf16[8,40,2048]{2,1,0:T(8,128)(2,1)} %copy.79), calls=%async_computation.1 | async-start | bytes 2621440 | tf_op jit(solution)/shard_map/all_to_all | solution.py:81
  234.5 20.5 %gather_fusion.2 = bf16[1280,2048]{1,0:T(8,128)(2,1)} fusion(bf16[4352,2048]{1,0:T(8,128)(2,1)} %all-gather.2.cloned.1.call-done, s32[2048]{0:T(1024)S(1)} %pad_clamp_fusion.1), kind=kCustom, calls=%fused_computation.2 | custom fusion | bytes 10490880 | tf_op jit(solution)/shard_map/jit(_take)/gather | solution.py:65
  255.0 7.9 %fusion.2 = f32[4,320,2,192]{1,3,0,2:T(8,128)S(1)} fusion(bf16[4,320,2048,1]{2,1,0,3:T(8,128)(2,1)} %bitcast.123, bf16[4,2,192,2048]{3,2,1,0:T(8,128)(2,1)} %get-tuple-element.25), kind=kOutput, calls=%fused_computation.8 | convolution fusion | flops 2013265920 | bytes 13500416 | tf_op jit(solution)/shard_map/jrd,jgfd->jrgf/dot_general | solution.py:67
  262.9 5.9 %convolution_convert_fusion.1 = bf16[4,320,2048]{2,1,0:T(8,128)(2,1)} fusion(bf16[16,192,2048]{2,1,0:T(8,128)(2,1)} %param.13, f32[4,320,2,192]{1,3,0,2:T(8,128)S(1)} %fusion.2), kind=kOutput, calls=%fused_computation.19 | convolution fusion | flops 1010728960 | bytes 10354688 | tf_op jit(solution)/shard_map/jrf,jfd->jrd/dot_general | solution.py:71
  268.8 9.1 %reduce-scatter.7.cloned.1.call-done = bf16[4,80,2048]{2,1,0:T(8,128)(2,1)} async-done(((bf16[4,320,2048]{2,1,0:T(8,128)(2,1)}), bf16[4,80,2048]{2,1,0:T(8,128)(2,1)}) %reduce-scatter.7.cloned.1.call-update) | async-done | bytes 1310736 | tf_op jit(solution)/shard_map/reduce_scatter | solution.py:77
  282.7 5.5 %all-to-all-start.1 = ((bf16[8,40,2048]{2,1,0:T(8,128)(2,1)}), bf16[8,40,2048]{2,1,0:T(8,128)(2,1)S(1)}, u32[]{:S(2)}, u32[]{:S(2)}) async-start(bf16[8,40,2048]{2,1,0:T(8,128)(2,1)} %copy.85), calls=%async_computation.3 | async-start | bytes 2621440 | tf_op jit(solution)/shard_map/all_to_all | solution.py:81
  288.8 20.2 %gather_fusion.3 = bf16[1280,2048]{1,0:T(8,128)(2,1)} fusion(bf16[4352,2048]{1,0:T(8,128)(2,1)} %all-gather.2.cloned.1.call-done, s32[2048]{0:T(1024)S(1)} %pad_clamp_fusion), kind=kCustom, calls=%fused_computation.3 | custom fusion | bytes 10490880 | tf_op jit(solution)/shard_map/jit(_take)/gather | solution.py:65
  309.0 7.9 %fusion = f32[4,320,2,192]{1,3,0,2:T(8,128)S(1)} fusion(bf16[4,320,2048,1]{2,1,0,3:T(8,128)(2,1)} %bitcast.121, bf16[4,2,192,2048]{3,2,1,0:T(8,128)(2,1)} %get-tuple-element.24), kind=kOutput, calls=%fused_computation.6 | convolution fusion | flops 2013265920 | bytes 13500416 | tf_op jit(solution)/shard_map/jrd,jgfd->jrgf/dot_general | solution.py:67
  316.9 5.9 %convolution_convert_fusion = bf16[4,320,2048]{2,1,0:T(8,128)(2,1)} fusion(bf16[16,192,2048]{2,1,0:T(8,128)(2,1)} %param.13, f32[4,320,2,192]{1,3,0,2:T(8,128)S(1)} %fusion), kind=kOutput, calls=%fused_computation.18 | convolution fusion | flops 1010728960 | bytes 10354688 | tf_op jit(solution)/shard_map/jrf,jfd->jrd/dot_general | solution.py:71
  322.8 8.8 %reduce-scatter.9.cloned.1.call-done = bf16[4,80,2048]{2,1,0:T(8,128)(2,1)} async-done(((bf16[4,320,2048]{2,1,0:T(8,128)(2,1)}), bf16[4,80,2048]{2,1,0:T(8,128)(2,1)}) %reduce-scatter.9.cloned.1.call-update) | async-done | bytes 1310736 | tf_op jit(solution)/shard_map/reduce_scatter | solution.py:77
  336.6 5.8 %all-to-all-start.2 = ((bf16[8,40,2048]{2,1,0:T(8,128)(2,1)}), bf16[8,40,2048]{2,1,0:T(8,128)(2,1)}, u32[]{:S(2)}, u32[]{:S(2)}) async-start(bf16[8,40,2048]{2,1,0:T(8,128)(2,1)} %copy.91), calls=%async_computation.5 | async-start | bytes 2621440 | tf_op jit(solution)/shard_map/all_to_all | solution.py:81
  342.4 43.3 %reduce-scatter.11.cloned.1.call-done = bf16[4,80,2048]{2,1,0:T(8,128)(2,1)} async-done(((bf16[4,320,2048]{2,1,0:T(8,128)(2,1)}), bf16[4,80,2048]{2,1,0:T(8,128)(2,1)}) %reduce-scatter.11.cloned.1.call-update) | async-done | bytes 1310736 | tf_op jit(solution)/shard_map/reduce_scatter | solution.py:77
  390.5 5.5 %all-to-all-start.3 = ((bf16[8,40,2048]{2,1,0:T(8,128)(2,1)}), bf16[8,40,2048]{2,1,0:T(8,128)(2,1)}, u32[]{:S(2)}, u32[]{:S(2)}) async-start(bf16[8,40,2048]{2,1,0:T(8,128)(2,1)} %copy.97), calls=%async_computation.7 | async-start | bytes 2621440 | tf_op jit(solution)/shard_map/all_to_all | solution.py:81
  396.5 31.9 %all-to-all-done.3 = bf16[8,40,2048]{2,1,0:T(8,128)(2,1)} async-done(((bf16[8,40,2048]{2,1,0:T(8,128)(2,1)}), bf16[8,40,2048]{2,1,0:T(8,128)(2,1)}, u32[]{:S(2)}, u32[]{:S(2)}) %all-to-all-start.3) | async-done | bytes 1310752 | tf_op jit(solution)/shard_map/all_to_all | solution.py:81
  428.4 6.0 %pad_maximum_fusion = bf16[8,160,2048]{2,1,0:T(8,128)(2,1)} fusion(bf16[8,40,2048]{2,1,0:T(8,128)(2,1)} %all-to-all-done.3, bf16[8,40,2048]{2,1,0:T(8,128)(2,1)} %all-to-all-done.2, bf16[8,40,2048]{2,1,0:T(8,128)(2,1)S(1)} %all-to-all-done.1, bf16[8,40,2048]{2,1,0:T(8,128)(2,1)S(1)} %all-to-all-done), kind=kLoop, calls=%fused_computation.14 | loop fusion | flops 20971520 | bytes 10485760 | tf_op jit(solution)/shard_map/concatenate | solution.py:83
  434.4 12.0 %gather_fusion.4 = bf16[1024,2048]{1,0:T(8,128)(2,1)} fusion(bf16[1280,2048]{1,0:T(8,128)(2,1)} %bitcast.120, s32[1024]{0:T(1024)S(1)} %broadcast_clamp_fusion), kind=kCustom, calls=%fused_computation.4 | custom fusion | bytes 8392704 | tf_op jit(solution)/shard_map/jit(_take)/gather | solution.py:84
  (91 shorter events, 37.7 us)
Async XLA Ops:
  6.5 8.4 %copy-start = (bf16[128,2048]{1,0:T(8,128)(2,1)S(1)}, bf16[128,2048]{1,0:T(8,128)(2,1)}, u32[]{:S(2)}) copy-start(bf16[128,2048]{1,0:T(8,128)(2,1)} %param.8) | copy-start | bytes 1572868
  6.5 8.5 %copy-start.5 = (f32[2048]{0:T(1024)S(1)}, f32[2048]{0:T(1024)}, u32[]{:S(2)}) copy-start(f32[2048]{0:T(1024)} %param.9) | copy-start | bytes 24580
  6.5 132.2 %all-gather.2.cloned.1.call-start = ((), (), s32[]{:S(2)}) async-start(), calls=%async_computation.8 | async-start | bytes 18382848 | tf_op jit(solution)/shard_map/all_gather | solution.py:51
  16.1 208.2 %reduce-scatter.5.cloned.1.call-start = ((), (), s32[]{:S(2)}) async-start(), calls=%async_computation.9 | async-start | bytes 6553600 | tf_op jit(solution)/shard_map/reduce_scatter | solution.py:77
  174.0 103.9 %reduce-scatter.7.cloned.1.call-start = ((), (), s32[]{:S(2)}) async-start(), calls=%async_computation.10 | async-start | bytes 6553600 | tf_op jit(solution)/shard_map/reduce_scatter | solution.py:77
  224.2 1.3 copy-start.2
  229.1 39.7 %all-to-all-start = ((bf16[8,40,2048]{2,1,0:T(8,128)(2,1)}), bf16[8,40,2048]{2,1,0:T(8,128)(2,1)S(1)}, u32[]{:S(2)}, u32[]{:S(2)}) async-start(bf16[8,40,2048]{2,1,0:T(8,128)(2,1)} %copy.79), calls=%async_computation.1 | async-start | bytes 2621440 | tf_op jit(solution)/shard_map/all_to_all | solution.py:81
  234.1 97.6 %reduce-scatter.9.cloned.1.call-start = ((), (), s32[]{:S(2)}) async-start(), calls=%async_computation.11 | async-start | bytes 6553600 | tf_op jit(solution)/shard_map/reduce_scatter | solution.py:77
  277.8 1.3 copy-start.1
  282.7 40.1 %all-to-all-start.1 = ((bf16[8,40,2048]{2,1,0:T(8,128)(2,1)}), bf16[8,40,2048]{2,1,0:T(8,128)(2,1)S(1)}, u32[]{:S(2)}, u32[]{:S(2)}) async-start(bf16[8,40,2048]{2,1,0:T(8,128)(2,1)} %copy.85), calls=%async_computation.3 | async-start | bytes 2621440 | tf_op jit(solution)/shard_map/all_to_all | solution.py:81
  288.2 97.4 %reduce-scatter.11.cloned.1.call-start = ((), (), s32[]{:S(2)}) async-start(), calls=%async_computation.12 | async-start | bytes 6553600 | tf_op jit(solution)/shard_map/reduce_scatter | solution.py:77
  336.6 53.9 %all-to-all-start.2 = ((bf16[8,40,2048]{2,1,0:T(8,128)(2,1)}), bf16[8,40,2048]{2,1,0:T(8,128)(2,1)}, u32[]{:S(2)}, u32[]{:S(2)}) async-start(bf16[8,40,2048]{2,1,0:T(8,128)(2,1)} %copy.91), calls=%async_computation.5 | async-start | bytes 2621440 | tf_op jit(solution)/shard_map/all_to_all | solution.py:81
  388.0 8.2 %copy-start.4 = (f32[128,8]{0,1:T(8,128)S(1)}, f32[128,8]{0,1:T(8,128)}, u32[]{:S(2)}) copy-start(f32[128,8]{0,1:T(8,128)} %param.11) | copy-start | bytes 12292
  388.0 8.4 %copy-start.3 = (s32[128,8]{0,1:T(8,128)S(1)}, s32[128,8]{0,1:T(8,128)}, u32[]{:S(2)}) copy-start(s32[128,8]{0,1:T(8,128)} %param.10) | copy-start | bytes 12292
  390.5 37.9 %all-to-all-start.3 = ((bf16[8,40,2048]{2,1,0:T(8,128)(2,1)}), bf16[8,40,2048]{2,1,0:T(8,128)(2,1)}, u32[]{:S(2)}, u32[]{:S(2)}) async-start(bf16[8,40,2048]{2,1,0:T(8,128)(2,1)} %copy.97), calls=%async_computation.7 | async-start | bytes 2621440 | tf_op jit(solution)/shard_map/all_to_all | solution.py:81
Sparse Core Ops, SparseCore 0:
  16.2 122.5 all-gather.1
  174.1 49.5 reduce-scatter.4
  226.4 51.4 reduce-scatter.6
  280.2 51.3 reduce-scatter.8
  334.2 51.3 reduce-scatter.10
where the time goes:
time: 467 us; the launch traced here: 458 us
  waiting for transfers between devices  216 us (46%)
  local copies, waits for them, and re-layouts  138 us (30%)
  matrix products  58.2 us (12%)
  starting transfers between devices  22.7 us (5%)
  between operations  13.7 us (3%)
  other arithmetic  9.89 us (2%)
    all_gather x1, waiting for transfers between devices, local(): every = lax.all_gather(packed, ALL, axis=0, tiled=True)  123 us
    gather x4, local copies, waits for them, and re-layouts, local(): picked = jnp.take(every, rows[span].reshape(-1), axis=0, mode='clip')  79.9 us
    reduce_scatter x4, waiting for transfers between devices, local(): lax.psum_scatter(partial, 'tok', scatter_dimension=1, tiled=True)  61.2 us
    all_to_all x4, waiting for transfers between devices, local(): lax.all_to_all(summed, ('row', 'col'), split_axis=0, concat_axis=0, tiled...  31.9 us
    dot_general x4, matrix products, local(): jnp.einsum('jrd,jgfd->jrgf', picked, gate_up_weight[span], preferred_elem...  31.4 us
    dot_general x4, matrix products, local(): jnp.einsum('jrf,jfd->jrd', hidden, down_weight[span], preferred_element_t...  23.3 us
    all_to_all x4, starting transfers between devices, local(): lax.all_to_all(summed, ('row', 'col'), split_axis=0, concat_axis=0, tiled...  21.7 us
    slice x1, local copies, waits for them, and re-layouts, local(): gate_up_weight[span]  16.3 us
  transfers between devices with their start and end apart: 9, of which 5 were waited for; matrix products, arithmetic and copies ran while one was open for 30% of the time, Pallas kernels for 0%

commit v1 on v0

--- a/solution.py
+++ b/solution.py
@@ -8,6 +8,28 @@
 PIECES = 4
 EPSILON = 1e-06
 ALL = ("row", "col", "tok")
+
+
+def split_up(value, dim, size):
+    before, after = (value.shape[:dim], value.shape[dim + 1 :])
+    return jnp.moveaxis(value.reshape(*before, size, -1, *after), dim, 0)
+
+
+def laid_out(pieces, dim):
+    pieces = jnp.moveaxis(pieces, 0, dim)
+    lengths = pieces.shape
+    return pieces.reshape(*lengths[:dim], lengths[dim] * lengths[dim + 1], *lengths[dim + 2 :])
+
+
+def pairwise_exchange(x, axis, split_dim, concat_dim):
+    size, here = (lax.axis_size(axis), lax.axis_index(axis))
+    parts = split_up(x, split_dim, size)
+    finished = [parts[here]]
+    for step in range(1, size):
+        sent = parts[here ^ step]
+        finished.append(lax.ppermute(sent, axis, [(i, i ^ step) for i in range(size)]))
+    parts = jnp.stack(finished)[here ^ jnp.arange(size)]
+    return laid_out(parts, concat_dim)
 
 
 def rank_in_block(block_routes, experts):
@@ -77,9 +99,7 @@
         sums.append(lax.psum_scatter(partial, "tok", scatter_dimension=1, tiled=True))
         summed = sums[-1].reshape(width, owners, CAP, features).transpose(1, 0, 2, 3)
         summed = summed.reshape(owners, width * CAP, features)
-        returned.append(
-            lax.all_to_all(summed, ("row", "col"), split_axis=0, concat_axis=0, tiled=True)
-        )
+        returned.append(pairwise_exchange(summed, ("row", "col"), 0, 0))
     returned = jnp.concatenate(returned, axis=1)
     picked_back = jnp.take(returned.reshape(experts * CAP, features), target, axis=0)
     picked_back = picked_back.reshape(count, chosen, features)

time: 467 us -> 501 us (1.073)
  local copies, waits for them, and re-layouts: 138 us -> 163 us
  starting transfers between devices: 22.7 us -> 47.5 us
  waiting for transfers between devices: 216 us -> 198 us
    ppermute x0 -> x28, waiting for transfers between devices: none -> 67.7 us  [pairwise_exchange(): lax.ppermute(sent, axis, [(i, i ^ step) for i in range(size)])]
    reduce_scatter x4, waiting for transfers between devices: 61.2 us -> 8.01 us  [local(): lax.psum_scatter(partial, 'tok', scatter_dimension=1, tiled=True)]
    ppermute x0 -> x28, starting transfers between devices: none -> 47.1 us  [pairwise_exchange(): lax.ppermute(sent, axis, [(i, i ^ step) for i in range(size)])]
    all_to_all x4 -> x0, waiting for transfers between devices: 31.9 us -> none  [local(): lax.all_to_all(summed, ('row', 'col'), split_axis=0, concat_axis=0, tiled...]
    all_to_all x4 -> x0, starting transfers between devices: 21.7 us -> none  [local(): lax.all_to_all(summed, ('row', 'col'), split_axis=0, concat_axis=0, tiled...]
    dynamic_slice x0 -> x4, local copies, waits for them, and re-layouts: none -> 12 us  [pairwise_exchange(): sent = parts[here ^ step]]
    unnamed x14 -> x72, local copies, waits for them, and re-layouts: 3.98 us -> 15.9 us
    gather x0 -> x4, local copies, waits for them, and re-layouts: none -> 8.62 us  [pairwise_exchange(): parts = jnp.stack(finished)[here ^ jnp.arange(size)]]
  transfers between devices with their start and end apart: 9 -> 33, of which waited for: 5 -> 13; matrix products, arithmetic and copies ran while one was open for 30% -> 31% of each run, Pallas kernels for 0% -> 0%
where the time goes in v1:
time: 501 us; the launch traced here: 493 us
  waiting for transfers between devices  198 us (40%)
  local copies, waits for them, and re-layouts  163 us (33%)
  matrix products  59.1 us (12%)
  starting transfers between devices  47.5 us (9%)
  between operations  14.4 us (3%)
  other arithmetic  9.89 us (2%)
    all_gather x1, waiting for transfers between devices, local(): every = lax.all_gather(packed, ALL, axis=0, tiled=True)  123 us
    gather x4, local copies, waits for them, and re-layouts, local(): picked = jnp.take(every, rows[span].reshape(-1), axis=0, mode='clip')  78.9 us
    ppermute x28, waiting for transfers between devices, pairwise_exchange(): lax.ppermute(sent, axis, [(i, i ^ step) for i in range(size)])  67.7 us
    ppermute x28, starting transfers between devices, pairwise_exchange(): lax.ppermute(sent, axis, [(i, i ^ step) for i in range(size)])  47.1 us
    dot_general x4, matrix products, local(): jnp.einsum('jrd,jgfd->jrgf', picked, gate_up_weight[span], preferred_elem...  32.2 us
    dot_general x4, matrix products, local(): jnp.einsum('jrf,jfd->jrd', hidden, down_weight[span], preferred_element_t...  23.4 us
    slice x1, local copies, waits for them, and re-layouts, local(): gate_up_weight[span]  16.3 us
    unnamed x72, local copies, waits for them, and re-layouts  15.9 us
  transfers between devices with their start and end apart: 33, of which 13 were waited for; matrix products, arithmetic and copies ran while one was open for 31% of the time, Pallas kernels for 0%

profile of v1, /device:TPU:0, one launch (start us, length us, event | category | flops | bytes accessed | tf_op | source)
XLA Modules:
  0.0 492.5 jit_solution(13999375871100387799)
XLA Ops:
  16.1 122.6 %all-gather.2.cloned.1.call-done = bf16[4352,2048]{1,0:T(8,128)(2,1)} async-done(((bf16[136,2048]{1,0:T(8,128)(2,1)}), bf16[4352,2048]{1,0:T(8,128)(2,1)}) %all-gather.2.cloned.1.call-update) | async-done | bytes 17825808 | tf_op jit(solution)/shard_map/all_gather | solution.py:73
  141.3 19.2 %gather_fusion = bf16[1280,2048]{1,0:T(8,128)(2,1)} fusion(bf16[4352,2048]{1,0:T(8,128)(2,1)} %all-gather.2.cloned.1.call-done, s32[2048]{0:T(1024)S(1)} %get-tuple-element.65), kind=kCustom, calls=%fused_computation | custom fusion | bytes 10490880 | tf_op jit(solution)/shard_map/jit(_take)/gather | solution.py:87
  160.5 7.8 %fusion.6 = f32[4,320,2,192]{1,3,2,0:T(8,128)S(1)} fusion(bf16[4,320,2048,1]{2,1,3,0:T(8,128)(2,1)} %bitcast.330, bf16[16,2,192,2048]{3,2,1,0:T(8,128)(2,1)} %param.12), kind=kOutput, calls=%fused_computation.16 | convolution fusion | flops 2013265920 | bytes 13500416 | tf_op jit(solution)/shard_map/jrd,jgfd->jrgf/dot_general | solution.py:89
  168.3 5.8 %convolution_convert_fusion.3 = bf16[4,320,2048]{2,1,0:T(8,128)(2,1)} fusion(bf16[16,192,2048]{2,1,0:T(8,128)(2,1)} %param.13, f32[4,320,2,192]{1,3,2,0:T(8,128)S(1)} %fusion.6), kind=kOutput, calls=%fused_computation.25 | convolution fusion | flops 1010728960 | bytes 10354688 | tf_op jit(solution)/shard_map/jrf,jfd->jrd/dot_general | solution.py:93
  174.4 16.3 %fusion.50 = (bf16[4,2,192,2048]{3,2,1,0:T(8,128)(2,1)}, bf16[4,2,192,2048]{3,2,1,0:T(8,128)(2,1)}, bf16[4,2,192,2048]{3,2,1,0:T(8,128)(2,1)}) fusion(bf16[16,2,192,2048]{3,2,1,0:T(8,128)(2,1)} %param.12), kind=kLoop, calls=%fused_computation.190 | loop fusion | bytes 37748736 | tf_op jit(solution)/shard_map/slice | solution.py:90
  190.7 20.1 %gather_fusion.2 = bf16[1280,2048]{1,0:T(8,128)(2,1)} fusion(bf16[4352,2048]{1,0:T(8,128)(2,1)} %all-gather.2.cloned.1.call-done, s32[2048]{0:T(1024)S(1)} %get-tuple-element.64), kind=kCustom, calls=%fused_computation.2 | custom fusion | bytes 10490880 | tf_op jit(solution)/shard_map/jit(_take)/gather | solution.py:87
  210.7 7.8 %fusion.4 = f32[4,320,2,192]{1,3,0,2:T(8,128)S(1)} fusion(bf16[4,320,2048,1]{2,1,0,3:T(8,128)(2,1)} %bitcast.328, bf16[4,2,192,2048]{3,2,1,0:T(8,128)(2,1)} %get-tuple-element.23), kind=kOutput, calls=%fused_computation.14 | convolution fusion | flops 2013265920 | bytes 13500416 | tf_op jit(solution)/shard_map/jrd,jgfd->jrgf/dot_general | solution.py:89
  218.5 5.7 %convolution_convert_fusion.2 = bf16[4,320,2048]{2,1,0:T(8,128)(2,1)} fusion(bf16[16,192,2048]{2,1,0:T(8,128)(2,1)} %param.13, f32[4,320,2,192]{1,3,0,2:T(8,128)S(1)} %fusion.4), kind=kOutput, calls=%fused_computation.24 | convolution fusion | flops 1010728960 | bytes 10354688 | tf_op jit(solution)/shard_map/jrf,jfd->jrd/dot_general | solution.py:93
  224.7 19.6 %gather_fusion.4 = bf16[1280,2048]{1,0:T(8,128)(2,1)} fusion(bf16[4352,2048]{1,0:T(8,128)(2,1)} %all-gather.2.cloned.1.call-done, s32[2048]{0:T(1024)S(1)} %get-tuple-element.63), kind=kCustom, calls=%fused_computation.4 | custom fusion | bytes 10490880 | tf_op jit(solution)/shard_map/jit(_take)/gather | solution.py:87
  244.3 8.7 %fusion.2 = f32[4,320,2,192]{1,3,0,2:T(8,128)S(1)} fusion(bf16[4,320,2048,1]{2,1,0,3:T(8,128)(2,1)} %bitcast.329, bf16[4,2,192,2048]{3,2,1,0:T(8,128)(2,1)} %get-tuple-element.25), kind=kOutput, calls=%fused_computation.12 | convolution fusion | flops 2013265920 | bytes 13500416 | tf_op jit(solution)/shard_map/jrd,jgfd->jrgf/dot_general | solution.py:89
  253.0 5.9 %convolution_convert_fusion.1 = bf16[4,320,2048]{2,1,0:T(8,128)(2,1)} fusion(bf16[16,192,2048]{2,1,0:T(8,128)(2,1)} %param.13, f32[4,320,2,192]{1,3,0,2:T(8,128)S(1)} %fusion.2), kind=kOutput, calls=%fused_computation.23 | convolution fusion | flops 1010728960 | bytes 10354688 | tf_op jit(solution)/shard_map/jrf,jfd->jrd/dot_general | solution.py:93
  275.3 4.9 collective-permute-done.1
  283.6 11.5 %collective-permute-done.5 = bf16[1,40,2048]{2,1,0:T(8,128)(2,1)S(1)} collective-permute-done((bf16[1,40,2048]{2,1,0:T(8,128)(2,1)S(1)}, bf16[1,40,2048]{2,1,0:T(8,128)(2,1)S(1)}, u32[]{:S(2)}, u32[]{:S(2)}) %collective-permute-start.5) | collective-permute-done | bytes 163872 | tf_op jit(solution)/shard_map/ppermute | solution.py:30
  295.8 20.1 %gather_fusion.6 = bf16[1280,2048]{1,0:T(8,128)(2,1)} fusion(bf16[4352,2048]{1,0:T(8,128)(2,1)} %all-gather.2.cloned.1.call-done, s32[2048]{0:T(1024)S(1)} %get-tuple-element.62), kind=kCustom, calls=%fused_computation.6 | custom fusion | bytes 10490880 | tf_op jit(solution)/shard_map/jit(_take)/gather | solution.py:87
  315.9 8.0 %fusion = f32[4,320,2,192]{1,3,0,2:T(8,128)S(1)} fusion(bf16[4,320,2048,1]{2,1,0,3:T(8,128)(2,1)} %bitcast.327, bf16[4,2,192,2048]{3,2,1,0:T(8,128)(2,1)} %get-tuple-element.24), kind=kOutput, calls=%fused_computation.10 | convolution fusion | flops 2013265920 | bytes 13500416 | tf_op jit(solution)/shard_map/jrd,jgfd->jrgf/dot_general | solution.py:89
  323.9 6.0 %convolution_convert_fusion = bf16[4,320,2048]{2,1,0:T(8,128)(2,1)} fusion(bf16[16,192,2048]{2,1,0:T(8,128)(2,1)} %param.13, f32[4,320,2,192]{1,3,0,2:T(8,128)S(1)} %fusion), kind=kOutput, calls=%fused_computation.22 | convolution fusion | flops 1010728960 | bytes 10354688 | tf_op jit(solution)/shard_map/jrf,jfd->jrd/dot_general | solution.py:93
  345.6 7.3 %collective-permute-done.8 = bf16[1,40,2048]{2,1,0:T(8,128)(2,1)S(1)} collective-permute-done((bf16[1,40,2048]{2,1,0:T(8,128)(2,1)S(1)}, bf16[1,40,2048]{2,1,0:T(8,128)(2,1)S(1)}, u32[]{:S(2)}, u32[]{:S(2)}) %collective-permute-start.8) | collective-permute-done | bytes 163872 | tf_op jit(solution)/shard_map/ppermute | solution.py:30
  355.3 10.5 %collective-permute-done.12 = bf16[1,40,2048]{2,1,0:T(8,128)(2,1)S(1)} collective-permute-done((bf16[1,40,2048]{2,1,0:T(8,128)(2,1)S(1)}, bf16[1,40,2048]{2,1,0:T(8,128)(2,1)S(1)}, u32[]{:S(2)}, u32[]{:S(2)}) %collective-permute-start.12) | collective-permute-done | bytes 163872 | tf_op jit(solution)/shard_map/ppermute | solution.py:30
  388.8 5.4 %collective-permute-done.15 = bf16[1,40,2048]{2,1,0:T(8,128)(2,1)S(1)} collective-permute-done((bf16[1,40,2048]{2,1,0:T(8,128)(2,1)S(1)}, bf16[1,40,2048]{2,1,0:T(8,128)(2,1)S(1)}, u32[]{:S(2)}, u32[]{:S(2)}) %collective-permute-start.15) | collective-permute-done | bytes 163872 | tf_op jit(solution)/shard_map/ppermute | solution.py:30
  400.2 7.8 %collective-permute-done.19 = bf16[1,40,2048]{2,1,0:T(8,128)(2,1)S(1)} collective-permute-done((bf16[1,40,2048]{2,1,0:T(8,128)(2,1)S(1)}, bf16[1,40,2048]{2,1,0:T(8,128)(2,1)S(1)}, u32[]{:S(2)}, u32[]{:S(2)}) %collective-permute-start.19) | collective-permute-done | bytes 163872 | tf_op jit(solution)/shard_map/ppermute | solution.py:30
  412.4 8.0 %reduce-scatter.11.cloned.1.call-done = bf16[4,80,2048]{2,1,0:T(8,128)(2,1)} async-done(((bf16[4,320,2048]{2,1,0:T(8,128)(2,1)}), bf16[4,80,2048]{2,1,0:T(8,128)(2,1)}) %reduce-scatter.11.cloned.1.call-update) | async-done | bytes 1310736 | tf_op jit(solution)/shard_map/reduce_scatter | solution.py:99
  449.7 8.9 %collective-permute-done.26 = bf16[1,40,2048]{2,1,0:T(8,128)(2,1)S(1)} collective-permute-done((bf16[1,40,2048]{2,1,0:T(8,128)(2,1)S(1)}, bf16[1,40,2048]{2,1,0:T(8,128)(2,1)S(1)}, u32[]{:S(2)}, u32[]{:S(2)}) %collective-permute-start.26) | collective-permute-done | bytes 163872 | tf_op jit(solution)/shard_map/ppermute | solution.py:30
  462.9 6.1 %pad_maximum_fusion = bf16[8,160,2048]{2,1,0:T(8,128)(2,1)} fusion(bf16[8,40,2048]{2,1,0:T(8,128)(2,1)} %gather_fusion.7, bf16[8,40,2048]{2,1,0:T(8,128)(2,1)} %gather_fusion.5, bf16[8,40,2048]{2,1,0:T(8,128)(2,1)S(1)} %gather_fusion.3, bf16[8,40,2048]{2,1,0:T(8,128)(2,1)S(1)} %gather_fusion.1), kind=kLoop, calls=%fused_computation.18 | loop fusion | flops 20971520 | bytes 10485760 | tf_op jit(solution)/shard_map/concatenate | solution.py:103
  469.0 12.0 %gather_fusion.8 = bf16[1024,2048]{1,0:T(8,128)(2,1)} fusion(bf16[1280,2048]{1,0:T(8,128)(2,1)} %bitcast.322, s32[1024]{0:T(1024)S(1)} %broadcast_clamp_fusion), kind=kCustom, calls=%fused_computation.8 | custom fusion | bytes 8392704 | tf_op jit(solution)/shard_map/jit(_take)/gather | solution.py:104
  (205 shorter events, 122.4 us)
Async XLA Ops:
  6.5 132.2 %all-gather.2.cloned.1.call-start = ((), (), s32[]{:S(2)}) async-start(), calls=%async_computation.4 | async-start | bytes 18382848 | tf_op jit(solution)/shard_map/all_gather | solution.py:73
  16.1 208.2 %reduce-scatter.5.cloned.1.call-start = ((), (), s32[]{:S(2)}) async-start(), calls=%async_computation.5 | async-start | bytes 6553600 | tf_op jit(solution)/shard_map/reduce_scatter | solution.py:99
  174.1 121.6 %reduce-scatter.7.cloned.1.call-start = ((), (), s32[]{:S(2)}) async-start(), calls=%async_computation.6 | async-start | bytes 6553600 | tf_op jit(solution)/shard_map/reduce_scatter | solution.py:99
  224.3 144.6 %reduce-scatter.9.cloned.1.call-start = ((), (), s32[]{:S(2)}) async-start(), calls=%async_computation.7 | async-start | bytes 6553600 | tf_op jit(solution)/shard_map/reduce_scatter | solution.py:99
  265.1 15.1 %collective-permute-start.1 = (bf16[1,40,2048]{2,1,0:T(8,128)(2,1)S(1)}, bf16[1,40,2048]{2,1,0:T(8,128)(2,1)S(1)}, u32[]{:S(2)}, u32[]{:S(2)}) collective-permute-start(bf16[1,40,2048]{2,1,0:T(8,128)(2,1)S(1)} %bitcast.360), channel_id=1, source_target_pairs={{0,8},{4,12},{8,0},{12,4},{16,24},{20,28},{24,16},{28,20},{1,9},{5... | collective-permute-start | bytes 491528 | tf_op jit(solution)/shard_map/ppermute | solution.py:30
  267.5 16.0 %collective-permute-start.2 = (bf16[1,40,2048]{2,1,0:T(8,128)(2,1)S(1)}, bf16[1,40,2048]{2,1,0:T(8,128)(2,1)S(1)}, u32[]{:S(2)}, u32[]{:S(2)}) collective-permute-start(bf16[1,40,2048]{2,1,0:T(8,128)(2,1)S(1)} %bitcast.348), channel_id=1, source_target_pairs={{0,12},{4,8},{8,4},{12,0},{16,28},{20,24},{24,20},{28,16},{1,13},{... | collective-permute-start | bytes 491528 | tf_op jit(solution)/shard_map/ppermute | solution.py:30
  268.6 14.9 %collective-permute-start.3 = (bf16[1,40,2048]{2,1,0:T(8,128)(2,1)S(1)}, bf16[1,40,2048]{2,1,0:T(8,128)(2,1)S(1)}, u32[]{:S(2)}, u32[]{:S(2)}) collective-permute-start(bf16[1,40,2048]{2,1,0:T(8,128)(2,1)S(1)} %bitcast.344), channel_id=1, source_target_pairs={{0,16},{4,20},{8,24},{12,28},{16,0},{20,4},{24,8},{28,12},{1,17},{... | collective-permute-start | bytes 491528 | tf_op jit(solution)/shard_map/ppermute | solution.py:30
  274.5 20.6 %collective-permute-start.5 = (bf16[1,40,2048]{2,1,0:T(8,128)(2,1)S(1)}, bf16[1,40,2048]{2,1,0:T(8,128)(2,1)S(1)}, u32[]{:S(2)}, u32[]{:S(2)}) collective-permute-start(bf16[1,40,2048]{2,1,0:T(8,128)(2,1)S(1)} %bitcast.356), channel_id=1, source_target_pairs={{0,24},{4,28},{8,16},{12,20},{16,8},{20,12},{24,0},{28,4},{1,25},{... | collective-permute-start | bytes 491528 | tf_op jit(solution)/shard_map/ppermute | solution.py:30
  280.2 14.9 %collective-permute-start.6 = (bf16[1,40,2048]{2,1,0:T(8,128)(2,1)S(1)}, bf16[1,40,2048]{2,1,0:T(8,128)(2,1)S(1)}, u32[]{:S(2)}, u32[]{:S(2)}) collective-permute-start(bf16[1,40,2048]{2,1,0:T(8,128)(2,1)S(1)} %bitcast.349), channel_id=1, source_target_pairs={{0,28},{4,24},{8,20},{12,16},{16,12},{20,8},{24,4},{28,0},{1,29},{... | collective-permute-start | bytes 491528 | tf_op jit(solution)/shard_map/ppermute | solution.py:30
  295.8 124.6 %reduce-scatter.11.cloned.1.call-start = ((), (), s32[]{:S(2)}) async-start(), calls=%async_computation.8 | async-start | bytes 6553600 | tf_op jit(solution)/shard_map/reduce_scatter | solution.py:99
  337.8 15.1 %collective-permute-start.8 = (bf16[1,40,2048]{2,1,0:T(8,128)(2,1)S(1)}, bf16[1,40,2048]{2,1,0:T(8,128)(2,1)S(1)}, u32[]{:S(2)}, u32[]{:S(2)}) collective-permute-start(bf16[1,40,2048]{2,1,0:T(8,128)(2,1)S(1)} %bitcast.361), channel_id=1, source_target_pairs={{0,8},{4,12},{8,0},{12,4},{16,24},{20,28},{24,16},{28,20},{1,9},{5... | collective-permute-start | bytes 491528 | tf_op jit(solution)/shard_map/ppermute | solution.py:30
  338.7 16.4 %collective-permute-start.9 = (bf16[1,40,2048]{2,1,0:T(8,128)(2,1)S(1)}, bf16[1,40,2048]{2,1,0:T(8,128)(2,1)S(1)}, u32[]{:S(2)}, u32[]{:S(2)}) collective-permute-start(bf16[1,40,2048]{2,1,0:T(8,128)(2,1)S(1)} %bitcast.350), channel_id=1, source_target_pairs={{0,12},{4,8},{8,4},{12,0},{16,28},{20,24},{24,20},{28,16},{1,13},{... | collective-permute-start | bytes 491528 | tf_op jit(solution)/shard_map/ppermute | solution.py:30
  344.1 21.7 %collective-permute-start.12 = (bf16[1,40,2048]{2,1,0:T(8,128)(2,1)S(1)}, bf16[1,40,2048]{2,1,0:T(8,128)(2,1)S(1)}, u32[]{:S(2)}, u32[]{:S(2)}) collective-permute-start(bf16[1,40,2048]{2,1,0:T(8,128)(2,1)S(1)} %bitcast.357), channel_id=1, source_target_pairs={{0,24},{4,28},{8,16},{12,20},{16,8},{20,12},{24,0},{28,4},{1,25},{... | collective-permute-start | bytes 491528 | tf_op jit(solution)/shard_map/ppermute | solution.py:30
  379.1 15.1 %collective-permute-start.15 = (bf16[1,40,2048]{2,1,0:T(8,128)(2,1)S(1)}, bf16[1,40,2048]{2,1,0:T(8,128)(2,1)S(1)}, u32[]{:S(2)}, u32[]{:S(2)}) collective-permute-start(bf16[1,40,2048]{2,1,0:T(8,128)(2,1)S(1)} %bitcast.362), channel_id=1, source_target_pairs={{0,8},{4,12},{8,0},{12,4},{16,24},{20,28},{24,16},{28,20},{1,9},{5... | collective-permute-start | bytes 491528 | tf_op jit(solution)/shard_map/ppermute | solution.py:30
  380.0 18.2 %collective-permute-start.16 = (bf16[1,40,2048]{2,1,0:T(8,128)(2,1)S(1)}, bf16[1,40,2048]{2,1,0:T(8,128)(2,1)S(1)}, u32[]{:S(2)}, u32[]{:S(2)}) collective-permute-start(bf16[1,40,2048]{2,1,0:T(8,128)(2,1)S(1)} %bitcast.352), channel_id=1, source_target_pairs={{0,12},{4,8},{8,4},{12,0},{16,28},{20,24},{24,20},{28,16},{1,13},{... | collective-permute-start | bytes 491528 | tf_op jit(solution)/shard_map/ppermute | solution.py:30
  381.5 17.4 %collective-permute-start.17 = (bf16[1,40,2048]{2,1,0:T(8,128)(2,1)S(1)}, bf16[1,40,2048]{2,1,0:T(8,128)(2,1)S(1)}, u32[]{:S(2)}, u32[]{:S(2)}) collective-permute-start(bf16[1,40,2048]{2,1,0:T(8,128)(2,1)S(1)} %bitcast.346), channel_id=1, source_target_pairs={{0,16},{4,20},{8,24},{12,28},{16,0},{20,4},{24,8},{28,12},{1,17},{... | collective-permute-start | bytes 491528 | tf_op jit(solution)/shard_map/ppermute | solution.py:30
  383.0 16.6 %collective-permute-start.18 = (bf16[1,40,2048]{2,1,0:T(8,128)(2,1)S(1)}, bf16[1,40,2048]{2,1,0:T(8,128)(2,1)S(1)}, u32[]{:S(2)}, u32[]{:S(2)}) collective-permute-start(bf16[1,40,2048]{2,1,0:T(8,128)(2,1)S(1)} %bitcast.342), channel_id=1, source_target_pairs={{0,20},{4,16},{8,28},{12,24},{16,4},{20,0},{24,12},{28,8},{1,21},{... | collective-permute-start | bytes 491528 | tf_op jit(solution)/shard_map/ppermute | solution.py:30
  385.0 23.0 %collective-permute-start.19 = (bf16[1,40,2048]{2,1,0:T(8,128)(2,1)S(1)}, bf16[1,40,2048]{2,1,0:T(8,128)(2,1)S(1)}, u32[]{:S(2)}, u32[]{:S(2)}) collective-permute-start(bf16[1,40,2048]{2,1,0:T(8,128)(2,1)S(1)} %bitcast.358), channel_id=1, source_target_pairs={{0,24},{4,28},{8,16},{12,20},{16,8},{20,12},{24,0},{28,4},{1,25},{... | collective-permute-start | bytes 491528 | tf_op jit(solution)/shard_map/ppermute | solution.py:30
  428.5 15.1 %collective-permute-start.22 = (bf16[1,40,2048]{2,1,0:T(8,128)(2,1)S(1)}, bf16[1,40,2048]{2,1,0:T(8,128)(2,1)S(1)}, u32[]{:S(2)}, u32[]{:S(2)}) collective-permute-start(bf16[1,40,2048]{2,1,0:T(8,128)(2,1)S(1)} %bitcast.363), channel_id=1, source_target_pairs={{0,8},{4,12},{8,0},{12,4},{16,24},{20,28},{24,16},{28,20},{1,9},{5... | collective-permute-start | bytes 491528 | tf_op jit(solution)/shard_map/ppermute | solution.py:30
  430.9 16.7 %collective-permute-start.23 = (bf16[1,40,2048]{2,1,0:T(8,128)(2,1)S(1)}, bf16[1,40,2048]{2,1,0:T(8,128)(2,1)S(1)}, u32[]{:S(2)}, u32[]{:S(2)}) collective-permute-start(bf16[1,40,2048]{2,1,0:T(8,128)(2,1)S(1)} %bitcast.354), channel_id=1, source_target_pairs={{0,12},{4,8},{8,4},{12,0},{16,28},{20,24},{24,20},{28,16},{1,13},{... | collective-permute-start | bytes 491528 | tf_op jit(solution)/shard_map/ppermute | solution.py:30
  431.4 16.9 %collective-permute-start.24 = (bf16[1,40,2048]{2,1,0:T(8,128)(2,1)S(1)}, bf16[1,40,2048]{2,1,0:T(8,128)(2,1)S(1)}, u32[]{:S(2)}, u32[]{:S(2)}) collective-permute-start(bf16[1,40,2048]{2,1,0:T(8,128)(2,1)S(1)} %bitcast.347), channel_id=1, source_target_pairs={{0,16},{4,20},{8,24},{12,28},{16,0},{20,4},{24,8},{28,12},{1,17},{... | collective-permute-start | bytes 491528 | tf_op jit(solution)/shard_map/ppermute | solution.py:30
  432.9 16.1 %collective-permute-start.25 = (bf16[1,40,2048]{2,1,0:T(8,128)(2,1)S(1)}, bf16[1,40,2048]{2,1,0:T(8,128)(2,1)S(1)}, u32[]{:S(2)}, u32[]{:S(2)}) collective-permute-start(bf16[1,40,2048]{2,1,0:T(8,128)(2,1)S(1)} %bitcast.343), channel_id=1, source_target_pairs={{0,20},{4,16},{8,28},{12,24},{16,4},{20,0},{24,12},{28,8},{1,21},{... | collective-permute-start | bytes 491528 | tf_op jit(solution)/shard_map/ppermute | solution.py:30
  436.6 21.9 %collective-permute-start.26 = (bf16[1,40,2048]{2,1,0:T(8,128)(2,1)S(1)}, bf16[1,40,2048]{2,1,0:T(8,128)(2,1)S(1)}, u32[]{:S(2)}, u32[]{:S(2)}) collective-permute-start(bf16[1,40,2048]{2,1,0:T(8,128)(2,1)S(1)} %bitcast.359), channel_id=1, source_target_pairs={{0,24},{4,28},{8,16},{12,20},{16,8},{20,12},{24,0},{28,4},{1,25},{... | collective-permute-start | bytes 491528 | tf_op jit(solution)/shard_map/ppermute | solution.py:30
  443.6 15.6 %collective-permute-start.27 = (bf16[1,40,2048]{2,1,0:T(8,128)(2,1)S(1)}, bf16[1,40,2048]{2,1,0:T(8,128)(2,1)S(1)}, u32[]{:S(2)}, u32[]{:S(2)}) collective-permute-start(bf16[1,40,2048]{2,1,0:T(8,128)(2,1)S(1)} %bitcast.355), channel_id=1, source_target_pairs={{0,28},{4,24},{8,20},{12,16},{16,12},{20,8},{24,4},{28,0},{1,29},{... | collective-permute-start | bytes 491528 | tf_op jit(solution)/shard_map/ppermute | solution.py:30
  (16 other events, 132.6 us)
Sparse Core Ops, SparseCore 0:
  16.2 122.5 all-gather.1
  174.3 49.5 reduce-scatter.4
  226.6 51.4 reduce-scatter.6
  295.9 50.3 reduce-scatter.8
  369.1 51.2 reduce-scatter.10
